TPU v7x, 256 devices: a whole 4x4x8 slice. The times are simulated.
256 devices in a mesh: rep: 8 (over y_hi, x), ep: 32 (over z, y_lo, core).
Axes of the slice: x: 4, y: 4 (y_hi: 2, y_lo: 2; y = y_hi * 2 + y_lo), z: 8, core: 2. Of those that a mesh axis runs over, the one named last changes fastest.
Arguments:
- queries: bfloat16 [8, 128, 36864], P('rep', None, 'ep'), may hold values from -64 to 64
- suffix_latent: bfloat16 [8, 73728], P('rep', 'ep'), may hold values from -4 to 4
- cache_pool: bfloat16 [8, 256, 36864], P('rep', 'ep'), may hold values from -4 to 4
- holders: int32 [8, 64], replicated, may hold values from 0 to 7, as said below
- block_slots: int32 [8, 64], replicated, may hold values from 0 to 7, as said below
- prefix_len: int32 [8], P('rep'), may hold values from 1024 to 4096, as said below
- hidden: bfloat16 [8, 128, 7168], P('rep', 'ep'), may hold values from -16 to 16
- w_value: bfloat16 [64, 512, 128], P('ep'), may hold values from -0.25 to 0.25
- w_out: bfloat16 [8192, 7168], P('ep'), may hold values from -0.0625 to 0.0625
- norm_gain: bfloat16 [7168], replicated, may hold values from 0.099609375 to 1.8984375
- experts: int32 [8, 128, 8], P('rep', 'ep'), may hold values from 0 to 31, all different within a row; in each aligned block of 4 rows (0 to 3, 4 to 7, ..., all dimensions but the last counted through in order) at most 2 rows name the same one
- gate_weights: bfloat16 [8, 128, 8], P('rep', 'ep'), may hold values from 0.029907227 to 0.29882812
- w_gate: bfloat16 [32, 7168, 1024], P('ep', None, 'rep'), may hold values from -0.0625 to 0.0625
- w_up: bfloat16 [32, 7168, 1024], P('ep', None, 'rep'), may hold values from -0.0625 to 0.0625
- w_down: bfloat16 [32, 1024, 7168], P('ep', 'rep'), may hold values from -0.1875 to 0.1875
Outputs:
- layer_out: float32 [8, 128, 7168], P('rep', 'ep')
Inputs may be any that keep to these rules, and one draw needn't show every extreme that they name: `holders`: for each group and each index s of ep, the blocks s * 2 to (s + 1) * 2 - 1 of its prefix come from holder groups none of which gives more than 1 of them. `block_slots`: block b of a prefix lies on index b // 2 of ep of its holder group. `prefix_len`: some group's prefix has 4096 tokens. Each row names 8 different experts; among the rows of one device no expert is named more than 2 times.
All inputs are finite; a program needn't handle non-finite values.
Results may differ from a plain program's by a relative error of at most 0.004.
Values may be sent and summed in bfloat16 or wider, within the bound.
No kernel may reach another device: no remote copies, remote signals or barrier semaphores. Data moves between devices by JAX's collectives and lax.ppermute only.
A program may use at most 128 MiB of HBM per device.

v0:
```python
import jax
import jax.numpy as jnp
from jax import lax
from jax.sharding import Mesh, PartitionSpec as P

KVR = 512
ROPE = 64
SUF = 128
EP = ("epo", "core")
score_scale = 0.07216878364870323
norm_eps = 1e-06


def expert_units(token_rows, gate_rows, up_rows):
    gate_part = jnp.dot(token_rows, gate_rows, preferred_element_type=jnp.float32)
    up_part = jnp.dot(token_rows, up_rows, preferred_element_type=jnp.float32)
    return (jax.nn.silu(gate_part) * up_part).astype(jnp.bfloat16)


def local(
    queries,
    suffix_latent,
    cache_pool,
    holders,
    block_slots,
    prefix_len,
    hidden,
    w_value,
    w_out,
    norm_gain,
    experts,
    gate_weights,
    w_gate,
    w_up,
    w_down,
):
    rep_count = lax.axis_size("rep")
    ep_count = lax.axis_size(EP)
    rep_index = lax.axis_index("rep")
    ep_index = lax.axis_index("epo") * lax.axis_size("core") + lax.axis_index("core")
    pool_count = cache_pool.shape[1]
    block_width = cache_pool.shape[2]
    per_device = holders.shape[1] // ep_count
    per_holder = (per_device + rep_count - 1) // rep_count
    latent_width = KVR + ROPE
    mine_holders = lax.dynamic_slice_in_dim(holders, ep_index * per_device, per_device, 1)
    mine_slots = lax.dynamic_slice_in_dim(block_slots, ep_index * per_device, per_device, 1)
    position = jnp.arange(per_device, dtype=jnp.int32)
    same_holder = mine_holders[:, :, None] == mine_holders[:, None, :]
    earlier = position[None, :] < position[:, None]
    occurrence = jnp.sum((same_holder & earlier[None, :, :]).astype(jnp.int32), axis=2)
    wanted = mine_holders == rep_index
    chosen_slot = occurrence[:, :, None] == jnp.arange(per_holder, dtype=jnp.int32)[None, None, :]
    chosen_row = mine_slots[:, :, None] == jnp.arange(pool_count, dtype=jnp.int32)[None, None, :]
    selector = jnp.einsum(
        "son,soh->snh",
        (wanted[:, :, None] & chosen_slot).astype(jnp.float32),
        chosen_row.astype(jnp.float32),
        precision=lax.Precision.HIGHEST,
    )
    outgoing = jnp.dot(
        selector.reshape(rep_count * per_holder, pool_count).astype(jnp.bfloat16),
        cache_pool[0],
        preferred_element_type=jnp.float32,
    )
    outgoing = outgoing.astype(jnp.bfloat16).reshape(rep_count, per_holder, block_width)
    incoming = lax.all_to_all(outgoing, "rep", split_axis=0, concat_axis=0, tiled=True)
    own_holders = lax.dynamic_index_in_dim(mine_holders, rep_index, 0, keepdims=False)
    own_order = lax.dynamic_index_in_dim(occurrence, rep_index, 0, keepdims=False)
    source = own_holders * per_holder + own_order
    picker = (
        source[:, None] == jnp.arange(rep_count * per_holder, dtype=jnp.int32)[None, :]
    ).astype(jnp.bfloat16)
    own_blocks = jnp.dot(
        picker,
        incoming.reshape(rep_count * per_holder, block_width),
        preferred_element_type=jnp.float32,
    ).astype(jnp.bfloat16)
    core_count = lax.axis_size("core")
    outer_count = ep_count // core_count
    pre_rows = per_device * (block_width // latent_width)
    suf_rows = SUF // ep_count
    pad_rows = -(pre_rows + suf_rows) % 16
    packed = jnp.concatenate(
        [
            own_blocks.reshape(pre_rows, latent_width),
            suffix_latent.reshape(suf_rows, latent_width),
            jnp.zeros((pad_rows, latent_width), own_blocks.dtype),
        ],
        axis=0,
    )
    row_count = packed.shape[0]
    chip_keys = lax.all_gather(packed[None], EP, axis=0, tiled=True)
    hidden_width, width = (w_down.shape[1], w_down.shape[2])
    chunk = width // rep_count
    down_cols = w_down[0].reshape(hidden_width, rep_count, chunk)
    down_cols = jnp.transpose(down_cols, (1, 0, 2))
    down_cols = lax.all_to_all(down_cols, "rep", 0, 0, tiled=True)
    gate_rows = lax.all_to_all(
        w_gate[0].reshape(rep_count, chunk, hidden_width), "rep", 0, 0, tiled=True
    )
    up_rows = lax.all_to_all(
        w_up[0].reshape(rep_count, chunk, hidden_width), "rep", 0, 0, tiled=True
    )
    chip_keys, down_cols, gate_rows, up_rows = lax.optimization_barrier(
        (chip_keys, down_cols, gate_rows, up_rows)
    )
    keys = chip_keys.reshape(-1, latent_width)
    device_of = lax.broadcasted_iota(jnp.int32, chip_keys.shape[:2], 0).reshape(-1)
    row_of = lax.broadcasted_iota(jnp.int32, chip_keys.shape[:2], 1).reshape(-1)
    is_prefix = (row_of < pre_rows) & (device_of * pre_rows + row_of < prefix_len[0])
    suffix_pos = device_of * suf_rows + row_of - pre_rows
    is_suffix = (row_of >= pre_rows) & (row_of < pre_rows + suf_rows)
    token_pos = jnp.arange(SUF, dtype=jnp.int32)
    visible = is_prefix[None, :] | is_suffix[None, :] & (suffix_pos[None, :] <= token_pos[:, None])
    query_rows = queries[0].reshape(SUF, -1, latent_width)
    scores = (
        jnp.einsum("thc,kc->htk", query_rows, keys, preferred_element_type=jnp.float32)
        * score_scale
    )
    scores = jnp.where(visible[None, :, :], scores, -1e30)
    highest = jnp.max(scores, axis=2)
    exps = jnp.exp(scores - highest[:, :, None])
    denominator = jnp.sum(exps, axis=2)
    latent = jnp.einsum(
        "htk,kc->thc", exps.astype(jnp.bfloat16), keys[:, :KVR], preferred_element_type=jnp.float32
    )
    latent = (latent / jnp.transpose(denominator)[:, :, None]).astype(jnp.bfloat16)
    head_values = jnp.einsum(
        "thc,hcv->thv", latent, w_value, preferred_element_type=jnp.float32
    ).astype(jnp.bfloat16)
    head_values = head_values.reshape(outer_count, core_count, suf_rows, -1)
    head_values = jnp.transpose(head_values, (1, 0, 2, 3)).reshape(SUF, -1)
    partial = jnp.dot(head_values, w_out, preferred_element_type=jnp.float32)
    partial = partial.reshape(core_count, SUF // core_count, -1)
    partial = lax.all_to_all(partial.astype(jnp.bfloat16), "core", 0, 0, tiled=True)
    partial = jnp.sum(partial.astype(jnp.float32), axis=0)
    partial = partial.reshape(outer_count, 16, -1).astype(jnp.bfloat16)
    attention = jnp.sum(
        lax.all_to_all(partial, "epo", 0, 0, tiled=True).astype(jnp.float32), axis=0
    )
    attention = attention.reshape(suf_rows, -1)
    residual = hidden[0].astype(jnp.float32) + attention
    scale_rows = lax.rsqrt(jnp.mean(residual * residual, axis=1, keepdims=True) + norm_eps)
    normed = (residual * scale_rows * norm_gain.astype(jnp.float32)).astype(jnp.bfloat16)
    tok_count = hidden.shape[1]
    chosen = experts[0]
    top_count = chosen.shape[1]
    expert_count = ep_count * w_gate.shape[0]
    capacity = min(tok_count, 2 * max(1, tok_count * top_count // expert_count))
    slot_count = expert_count * capacity
    flat_choice = chosen.reshape(-1)
    hits = (flat_choice[:, None] == jnp.arange(expert_count, dtype=jnp.int32)[None, :]).astype(
        jnp.int32
    )
    rank = jnp.sum((jnp.cumsum(hits, axis=0) - hits) * hits, axis=1)
    slot_id = flat_choice * capacity + rank
    slot_hot = (slot_id[:, None] == jnp.arange(slot_count, dtype=jnp.int32)[None, :]).astype(
        jnp.float32
    )
    owner = jnp.arange(flat_choice.shape[0], dtype=jnp.int32) // top_count
    token_hot = (owner[:, None] == jnp.arange(tok_count, dtype=jnp.int32)[None, :]).astype(
        jnp.float32
    )
    placing = jnp.dot(jnp.transpose(slot_hot), token_hot, precision=lax.Precision.HIGHEST)
    weighted_hot = token_hot * gate_weights[0].astype(jnp.float32).reshape(-1)[:, None]
    combine = jnp.dot(jnp.transpose(weighted_hot), slot_hot, precision=lax.Precision.HIGHEST)
    grouped = jnp.dot(
        placing.astype(jnp.bfloat16), normed, preferred_element_type=jnp.float32
    ).astype(jnp.bfloat16)
    width = grouped.shape[1]
    spread = grouped.reshape(expert_count, capacity, rep_count, chunk)
    spread = jnp.transpose(spread, (2, 0, 1, 3)).reshape(rep_count * expert_count, capacity, chunk)
    columns = lax.all_to_all(spread, ("rep",) + EP, 0, 0, tiled=True).reshape(-1, chunk)
    gate_part = jnp.einsum("nd,rdk->rnk", columns, gate_rows, preferred_element_type=jnp.float32)
    up_part = jnp.einsum("nd,rdk->rnk", columns, up_rows, preferred_element_type=jnp.float32)
    parts = jnp.concatenate([gate_part, up_part], axis=2).astype(jnp.bfloat16)
    parts = lax.all_to_all(parts, "rep", 0, 0, tiled=True)
    sums = jnp.sum(parts.astype(jnp.float32), axis=0)
    gate_sum, up_sum = (sums[:, :hidden_width], sums[:, hidden_width:])
    units = (jax.nn.silu(gate_sum) * up_sum).astype(jnp.bfloat16)
    hidden_width = units.shape[1]
    unit_copies = jnp.broadcast_to(units[None], (rep_count,) + units.shape)
    units_all = lax.all_to_all(unit_copies, "rep", 0, 0, tiled=True)
    pieces = jnp.einsum("rnk,rkc->rnc", units_all, down_cols, preferred_element_type=jnp.float32)
    out_cols = jnp.sum(pieces.astype(jnp.bfloat16).astype(jnp.float32), axis=0)
    out_cols = out_cols.astype(jnp.bfloat16)
    out_cols = out_cols.reshape(rep_count * expert_count, capacity, chunk)
    back = lax.all_to_all(out_cols, ("rep",) + EP, 0, 0, tiled=True)
    back = back.reshape(rep_count, expert_count, capacity, chunk)
    served = jnp.transpose(back, (1, 2, 0, 3))
    mixture = jnp.dot(
        combine,
        served.reshape(slot_count, width).astype(jnp.float32),
        precision=lax.Precision.HIGHEST,
    )
    return (residual + mixture)[None]


def solution(mesh):
    rep_n, ep_n = mesh.devices.shape
    fine = Mesh(mesh.devices.reshape(rep_n, ep_n // 2, 2), ("rep", "epo", "core"))
    return jax.shard_map(
        local,
        mesh=fine,
        in_specs=(
            P("rep", None, EP),
            P("rep", EP),
            P("rep", EP, None),
            P(),
            P(),
            P("rep"),
            P("rep", EP, None),
            P(EP, None, None),
            P(EP, None),
            P(),
            P("rep", EP, None),
            P("rep", EP, None),
            P(EP, None, "rep"),
            P(EP, None, "rep"),
            P(EP, "rep", None),
        ),
        out_specs=P("rep", EP, None),
        check_vma=False,
    )
```

profile of v0, /device:TPU:1, one launch (start us, length us, event | category | flops | bytes accessed | tf_op | source)
XLA Modules:
  0.0 342.8 jit_solution(10226278535675166483)
XLA Ops:
  9.8 1.2 reshape.261
  11.0 7.5 %all-to-all-start = ((bf16[8,2,18432]{2,1,0:T(2,128)(2,1)}), bf16[8,2,18432]{2,1,0:T(2,128)(2,1)S(1)}, u32[]{:S(2)}, u32[]{:S(2)}) async-start(bf16[8,2,18432]{2,1,0:T(2,128)(2,1)} %reshape.261), calls=%async_computation | async-start | bytes 1179648 | tf_op jit(solution)/shard_map/all_to_all | solution.py:67
  19.8 11.1 %all-to-all-done = bf16[8,2,18432]{2,1,0:T(2,128)(2,1)S(1)} async-done(((bf16[8,2,18432]{2,1,0:T(2,128)(2,1)}), bf16[8,2,18432]{2,1,0:T(2,128)(2,1)S(1)}, u32[]{:S(2)}, u32[]{:S(2)}) %all-to-all-start) | async-done | bytes 589856 | tf_op jit(solution)/shard_map/all_to_all | solution.py:67
  33.2 1.8 copy.140
  35.1 1.6 copy.150
  36.7 4.4 %all-to-all-start.1 = ((bf16[8,128,896]{2,1,0:T(8,128)(2,1)}), bf16[8,128,896]{2,1,0:T(8,128)(2,1)}, u32[]{:S(2)}, u32[]{:S(2)}) async-start(bf16[8,128,896]{2,1,0:T(8,128)(2,1)} %bitcast.95), calls=%async_computation.1 | async-start | bytes 3670016 | tf_op jit(solution)/shard_map/all_to_all | solution.py:98
  41.1 2.7 copy.115
  43.8 23.2 %all-to-all-done.1 = bf16[8,128,896]{2,1,0:T(8,128)(2,1)} async-done(((bf16[8,128,896]{2,1,0:T(8,128)(2,1)}), bf16[8,128,896]{2,1,0:T(8,128)(2,1)}, u32[]{:S(2)}, u32[]{:S(2)}) %all-to-all-start.1) | async-done | bytes 1835040 | tf_op jit(solution)/shard_map/all_to_all | solution.py:98
  67.0 6.8 %all-to-all-start.2 = ((bf16[8,896,128]{1,2,0:T(8,128)(2,1)}), bf16[8,896,128]{1,2,0:T(8,128)(2,1)}, u32[]{:S(2)}, u32[]{:S(2)}) async-start(bf16[8,896,128]{1,2,0:T(8,128)(2,1)} %copy.115), calls=%async_computation.2 | async-start | bytes 3670016 | tf_op jit(solution)/shard_map/all_to_all | solution.py:99
  73.8 2.7 copy.116
  76.5 25.9 %all-to-all-done.2 = bf16[8,896,128]{1,2,0:T(8,128)(2,1)} async-done(((bf16[8,896,128]{1,2,0:T(8,128)(2,1)}), bf16[8,896,128]{1,2,0:T(8,128)(2,1)}, u32[]{:S(2)}, u32[]{:S(2)}) %all-to-all-start.2) | async-done | bytes 1835040 | tf_op jit(solution)/shard_map/all_to_all | solution.py:99
  102.3 4.4 %all-to-all-start.3 = ((bf16[8,896,128]{1,2,0:T(8,128)(2,1)}), bf16[8,896,128]{1,2,0:T(8,128)(2,1)S(1)}, u32[]{:S(2)}, u32[]{:S(2)}) async-start(bf16[8,896,128]{1,2,0:T(8,128)(2,1)} %copy.116), calls=%async_computation.3 | async-start | bytes 3670016 | tf_op jit(solution)/shard_map/all_to_all | solution.py:102
  108.0 3.9 %fusion.11 = pred[128,4608]{0,1:T(8,128)(4,1)S(1)} fusion(s32[4608]{0:T(1024)S(1)} %sub.25, pred[4608]{0:T(1024)(128)(4,1)S(1)} %and.68, pred[4608]{0:T(1024)(128)(4,1)S(1)} %and.66), kind=kLoop, calls=%fused_computation.21 | loop fusion | flops 1769472 | bytes 617472 | tf_op jit(solution)/shard_map/or | solution.py:115
  111.9 22.9 %all-to-all-done.3 = bf16[8,896,128]{1,2,0:T(8,128)(2,1)S(1)} async-done(((bf16[8,896,128]{1,2,0:T(8,128)(2,1)}), bf16[8,896,128]{1,2,0:T(8,128)(2,1)S(1)}, u32[]{:S(2)}, u32[]{:S(2)}) %all-to-all-start.3) | async-done | bytes 1835040 | tf_op jit(solution)/shard_map/all_to_all | solution.py:102
  134.8 9.8 %all-gather.3.cloned.1.call-done = bf16[4608,576]{1,0:T(8,128)(2,1)} async-done(((bf16[144,576]{1,0:T(8,128)(2,1)}), bf16[4608,576]{1,0:T(8,128)(2,1)}) %all-gather.3.cloned.1.call-update) | async-done | bytes 5308432 | tf_op jit(solution)/shard_map/all_gather | solution.py:93
  144.6 4.7 %fusion.57 = (f32[2,128]{1,0:T(2,128)S(1)}, f32[2,128,4608]{1,2,0:T(8,128)S(1)}) fusion(bf16[4608,576,1]{1,0,2:T(8,128)(2,1)} %bitcast.112, bf16[128,2,576]{0,2,1:T(8,128)(2,1)S(1)} %bitcast.107, pred[128,4608]{0,1:T(8,128)(4,1)S(1)} %fusion.11), kind=kOutput, calls=%fused_computation.92 | convolution fusion | flops 1362493184 | bytes 10912768 | tf_op jit(solution)/shard_map/thc,kc->htk/dot_general | solution.py:118
  150.0 1.5 copy-done.1
  151.5 5.5 %fusion.17 = bf16[128,2,128]{2,0,1:T(8,128)(2,1)S(1)} fusion(bf16[2,512,128]{2,1,0:T(8,128)(2,1)S(1)} %copy-done.11, f32[2,128,4608]{1,2,0:T(8,128)} %copy-done.1, f32[2,128]{1,0:T(2,128)S(1)} %get-tuple-element.13, bf16[4608,576]{1,0:T(8,128)(2,1)} %all-gather.3.cloned.1.call-done, f32[128,2]{0,1:T(2,128)S(1)} %bitcast.111), kind=kOutput, calls=%fused_computation.31 | convolution fusion | flops 1244168192 | bytes 9766912 | tf_op jit(solution)/shard_map/thc,hcv->thv/dot_general | solution.py:129
  157.2 2.7 convolution_convert_fusion.2
  159.9 5.2 %all_to_all.50 = bf16[2,64,7168]{2,1,0:T(8,128)(2,1)S(1)} all-to-all(bf16[2,64,7168]{2,1,0:T(8,128)(2,1)S(1)} %convolution_convert_fusion.2), channel_id=1, replica_groups=mesh['rep'=8,'epo'=16,'core'=2] {'core'}, dimensions={0} | all-to-all | bytes 3670016 | tf_op jit(solution)/shard_map/all_to_all | solution.py:136
  165.9 1.5 convert_element_type.105
  167.4 6.4 %all-to-all-start.5 = ((bf16[16,16,1792]{2,1,0:T(8,128)(2,1)}), bf16[16,16,1792]{2,1,0:T(8,128)(2,1)S(1)}, u32[]{:S(2)}, u32[]{:S(2)}) async-start(bf16[16,16,1792]{2,1,0:T(8,128)(2,1)} %convert_element_type.105), calls=%async_computation.5 | async-start | bytes 1835008 | tf_op jit(solution)/shard_map/all_to_all | solution.py:140
  174.6 22.5 %all-to-all-done.5 = bf16[16,16,1792]{2,1,0:T(8,128)(2,1)S(1)} async-done(((bf16[16,16,1792]{2,1,0:T(8,128)(2,1)}), bf16[16,16,1792]{2,1,0:T(8,128)(2,1)S(1)}, u32[]{:S(2)}, u32[]{:S(2)}) %all-to-all-start.5) | async-done | bytes 917536 | tf_op jit(solution)/shard_map/all_to_all | solution.py:140
  199.5 39.4 %all_to_all.51 = bf16[256,2,896]{2,1,0:T(2,128)(2,1)S(1)} all-to-all(bf16[256,2,896]{2,1,0:T(2,128)(2,1)S(1)} %copy.126), channel_id=1, replica_groups=mesh['rep'=8,'epo'=16,'core'=2] {'rep','epo','core'}, dimensions={0} | all-to-all | bytes 1835008 | tf_op jit(solution)/shard_map/all_to_all | solution.py:174
  239.2 2.9 fusion.12
  242.1 1.3 fusion.13
  243.6 31.2 %all_to_all.52 = bf16[8,512,256]{1,2,0:T(8,128)(2,1)S(1)} all-to-all(bf16[8,512,256]{1,2,0:T(8,128)(2,1)S(1)} %pad_maximum_fusion), channel_id=1, replica_groups=mesh['rep'=8,'epo'=16,'core'=2] {'rep'}, dimensions={0} | all-to-all | bytes 4194304 | tf_op jit(solution)/shard_map/all_to_all | solution.py:178
  275.5 17.4 %all_to_all.53 = bf16[8,512,128]{2,1,0:T(8,128)(2,1)S(1)} all-to-all(bf16[8,512,128]{2,1,0:T(8,128)(2,1)S(1)} %broadcast_in_dim.20), channel_id=1, replica_groups=mesh['rep'=8,'epo'=16,'core'=2] {'rep'}, dimensions={0} | all-to-all | bytes 2097152 | tf_op jit(solution)/shard_map/all_to_all | solution.py:184
  292.8 3.6 %convert_reduce_fusion = bf16[512,896]{1,0:T(8,128)(2,1)S(1)} fusion(bf16[8,512,128]{2,1,0:T(8,128)(2,1)S(1)} %all_to_all.53, bf16[8,128,896]{2,1,0:T(8,128)(2,1)} %all-to-all-done.1), kind=kOutput, calls=%fused_computation.7 | convolution fusion | flops 946405376 | bytes 3801088 | tf_op jit(solution)/shard_map/rnk,rkc->rnc/dot_general | solution.py:185
  296.5 1.3 reshape.245
  297.8 8.3 %all-to-all-start.9 = ((bf16[256,2,896]{2,1,0:T(2,128)(2,1)}), bf16[256,2,896]{2,1,0:T(2,128)(2,1)S(1)}, u32[]{:S(2)}, u32[]{:S(2)}) async-start(bf16[256,2,896]{2,1,0:T(2,128)(2,1)} %reshape.245), calls=%async_computation.9 | async-start | bytes 1835008 | tf_op jit(solution)/shard_map/all_to_all | solution.py:189
  306.4 27.8 %all-to-all-done.9 = bf16[256,2,896]{2,1,0:T(2,128)(2,1)S(1)} async-done(((bf16[256,2,896]{2,1,0:T(2,128)(2,1)}), bf16[256,2,896]{2,1,0:T(2,128)(2,1)S(1)}, u32[]{:S(2)}, u32[]{:S(2)}) %all-to-all-start.9) | async-done | bytes 917536 | tf_op jit(solution)/shard_map/all_to_all | solution.py:189
  (90 shorter events, 15.1 us)
Async XLA Ops:
  6.5 1.3 copy-start
  7.9 11.6 %copy-start.9 = (bf16[1,2304]{1,0:T(2,128)(2,1)S(1)}, bf16[1,2304]{1,0:T(2,128)(2,1)}, u32[]{:S(2)}) copy-start(bf16[1,2304]{1,0:T(2,128)(2,1)} %param.16) | copy-start | bytes 13828
  11.0 19.9 %all-to-all-start = ((bf16[8,2,18432]{2,1,0:T(2,128)(2,1)}), bf16[8,2,18432]{2,1,0:T(2,128)(2,1)S(1)}, u32[]{:S(2)}, u32[]{:S(2)}) async-start(bf16[8,2,18432]{2,1,0:T(2,128)(2,1)} %reshape.261), calls=%async_computation | async-start | bytes 1179648 | tf_op jit(solution)/shard_map/all_to_all | solution.py:67
  18.5 126.0 %all-gather.3.cloned.1.call-start = ((), (), s32[]{:S(2)}) async-start(), calls=%async_computation.10 | async-start | bytes 6082560 | tf_op jit(solution)/shard_map/all_gather | solution.py:93
  36.7 4.5 %copy-start.2 = (bf16[1,7168,128]{2,1,0:T(8,128)(2,1)S(1)}, bf16[1,7168,128]{2,1,0:T(8,128)(2,1)}, u32[]{:S(2)}) copy-start(bf16[1,7168,128]{2,1,0:T(8,128)(2,1)} %param.27) | copy-start | bytes 5505028
  36.7 30.3 %all-to-all-start.1 = ((bf16[8,128,896]{2,1,0:T(8,128)(2,1)}), bf16[8,128,896]{2,1,0:T(8,128)(2,1)}, u32[]{:S(2)}, u32[]{:S(2)}) async-start(bf16[8,128,896]{2,1,0:T(8,128)(2,1)} %bitcast.95), calls=%async_computation.1 | async-start | bytes 3670016 | tf_op jit(solution)/shard_map/all_to_all | solution.py:98
  43.8 30.0 %copy-start.3 = (bf16[1,7168,128]{2,1,0:T(8,128)(2,1)S(1)}, bf16[1,7168,128]{2,1,0:T(8,128)(2,1)}, u32[]{:S(2)}) copy-start(bf16[1,7168,128]{2,1,0:T(8,128)(2,1)} %param.28) | copy-start | bytes 5505028
  67.0 35.4 %all-to-all-start.2 = ((bf16[8,896,128]{1,2,0:T(8,128)(2,1)}), bf16[8,896,128]{1,2,0:T(8,128)(2,1)}, u32[]{:S(2)}, u32[]{:S(2)}) async-start(bf16[8,896,128]{1,2,0:T(8,128)(2,1)} %copy.115), calls=%async_computation.2 | async-start | bytes 3670016 | tf_op jit(solution)/shard_map/all_to_all | solution.py:99
  76.5 31.3 %copy-start.7 = (bf16[1,128,1152]{2,1,0:T(8,128)(2,1)S(1)}, bf16[1,128,1152]{2,1,0:T(8,128)(2,1)}, u32[]{:S(2)}) copy-start(bf16[1,128,1152]{2,1,0:T(8,128)(2,1)} %param.15) | copy-start | bytes 884740
  102.3 32.4 %all-to-all-start.3 = ((bf16[8,896,128]{1,2,0:T(8,128)(2,1)}), bf16[8,896,128]{1,2,0:T(8,128)(2,1)S(1)}, u32[]{:S(2)}, u32[]{:S(2)}) async-start(bf16[8,896,128]{1,2,0:T(8,128)(2,1)} %copy.116), calls=%async_computation.3 | async-start | bytes 3670016 | tf_op jit(solution)/shard_map/all_to_all | solution.py:102
  134.8 14.5 %copy-start.4 = (bf16[8,896,128]{1,2,0:T(8,128)(2,1)}, bf16[8,896,128]{1,2,0:T(8,128)(2,1)S(1)}, u32[]{:S(2)}) copy-start(bf16[8,896,128]{1,2,0:T(8,128)(2,1)S(1)} %all-to-all-done.3) | copy-start | bytes 5505028
  149.3 2.2 copy-start.1
  149.3 2.2 copy-start.11
  165.9 8.0 %copy-start.6 = (bf16[1,4,7168]{2,1,0:T(4,128)(2,1)S(1)}, bf16[1,4,7168]{2,1,0:T(4,128)(2,1)}, u32[]{:S(2)}) copy-start(bf16[1,4,7168]{2,1,0:T(4,128)(2,1)} %param.21) | copy-start | bytes 172036
  165.9 8.1 %copy-start.10 = (s32[1,4,8]{2,1,0:T(4,128)S(1)}, s32[1,4,8]{2,1,0:T(4,128)}, u32[]{:S(2)}) copy-start(s32[1,4,8]{2,1,0:T(4,128)} %param.25) | copy-start | bytes 388
  165.9 8.3 %copy-start.8 = (bf16[7168]{0:T(1024)(128)(2,1)S(1)}, bf16[7168]{0:T(1024)(128)(2,1)}, u32[]{:S(2)}) copy-start(bf16[7168]{0:T(1024)(128)(2,1)} %param.24) | copy-start | bytes 43012
  167.4 29.7 %all-to-all-start.5 = ((bf16[16,16,1792]{2,1,0:T(8,128)(2,1)}), bf16[16,16,1792]{2,1,0:T(8,128)(2,1)S(1)}, u32[]{:S(2)}, u32[]{:S(2)}) async-start(bf16[16,16,1792]{2,1,0:T(8,128)(2,1)} %convert_element_type.105), calls=%async_computation.5 | async-start | bytes 1835008 | tf_op jit(solution)/shard_map/all_to_all | solution.py:140
  239.2 2.9 copy-start.5
  296.5 9.6 %copy-start.12 = (bf16[1,4,8]{2,1,0:T(4,128)(2,1)S(1)}, bf16[1,4,8]{2,1,0:T(4,128)(2,1)}, u32[]{:S(2)}) copy-start(bf16[1,4,8]{2,1,0:T(4,128)(2,1)} %param.26) | copy-start | bytes 196
  297.8 36.5 %all-to-all-start.9 = ((bf16[256,2,896]{2,1,0:T(2,128)(2,1)}), bf16[256,2,896]{2,1,0:T(2,128)(2,1)S(1)}, u32[]{:S(2)}, u32[]{:S(2)}) async-start(bf16[256,2,896]{2,1,0:T(2,128)(2,1)} %reshape.245), calls=%async_computation.9 | async-start | bytes 1835008 | tf_op jit(solution)/shard_map/all_to_all | solution.py:189
Sparse Core Ops, SparseCore 0:
  33.4 111.1 all-gather.2
where the time goes:
time: 344 us; the launch traced here: 343 us
  waiting for transfers between devices  143 us (42%)
  blocking collectives  93.1 us (27%)
  starting transfers between devices  38 us (11%)
  matrix products  24.1 us (7%)
  local copies, waits for them, and re-layouts  21.1 us (6%)
  between operations  14.5 us (4%)
  other arithmetic  8.76 us (3%)
    all_to_all x1, blocking collectives, local(): lax.all_to_all(spread, ('rep',) + EP, 0, 0, tiled=True).reshape(-1, chunk)  39.4 us
    all_to_all x1, blocking collectives, local(): parts = lax.all_to_all(parts, 'rep', 0, 0, tiled=True)  31.2 us
    all_to_all x1, waiting for transfers between devices, local(): back = lax.all_to_all(out_cols, ('rep',) + EP, 0, 0, tiled=True)  27.8 us
    all_to_all x1, waiting for transfers between devices, local(): lax.all_to_all(w_gate[0].reshape(rep_count, chunk, hidden_width), 'rep',...  25.9 us
    all_to_all x1, waiting for transfers between devices, local(): down_cols = lax.all_to_all(down_cols, 'rep', 0, 0, tiled=True)  23.2 us
    all_to_all x1, waiting for transfers between devices, local(): lax.all_to_all(w_up[0].reshape(rep_count, chunk, hidden_width), 'rep', 0,...  22.9 us
    all_to_all x1, waiting for transfers between devices, local(): lax.all_to_all(partial, 'epo', 0, 0, tiled=True).astype(jnp.float32)  22.5 us
    all_to_all x1, blocking collectives, local(): units_all = lax.all_to_all(unit_copies, 'rep', 0, 0, tiled=True)  17.4 us
  transfers between devices with their start and end apart: 7, of which 7 were waited for; matrix products, arithmetic and copies ran while one was open for 5% of the time, Pallas kernels for 0%

commit v1 on v0

--- a/solution.py
+++ b/solution.py
@@ -90,7 +90,9 @@
         axis=0,
     )
     row_count = packed.shape[0]
-    chip_keys = lax.all_gather(packed[None], EP, axis=0, tiled=True)
+    chip_keys = jnp.concatenate(
+        lax.all_to_all(jnp.stack([packed[None]] * lax.axis_size(EP)), EP, 0, 0), axis=0
+    )
     hidden_width, width = (w_down.shape[1], w_down.shape[2])
     chunk = width // rep_count
     down_cols = w_down[0].reshape(hidden_width, rep_count, chunk)

time: 344 us -> 450 us (1.31)
  waiting for transfers between devices: 143 us -> 258 us
  between operations: 14.5 us -> 1.13 us
    all_to_all x0 -> x1, waiting for transfers between devices: none -> 128 us  [local(): lax.all_to_all(jnp.stack([packed[None]] * lax.axis_size(EP)), EP, 0, 0)]
    all_gather x1 -> x0, waiting for transfers between devices: 9.79 us -> none  [local(): chip_keys = lax.all_gather(packed[None], EP, axis=0, tiled=True)]
    all_to_all x0 -> x1, starting transfers between devices: none -> 9.73 us  [local(): lax.all_to_all(jnp.stack([packed[None]] * lax.axis_size(EP)), EP, 0, 0)]
  transfers between devices with their start and end apart: 7 -> 7, of which waited for: 7 -> 7; matrix products, arithmetic and copies ran while one was open for 5% -> 3% of each run, Pallas kernels for 0% -> 0%
where the time goes in v1:
time: 450 us; the launch traced here: 449 us
  waiting for transfers between devices  258 us (57%)
  blocking collectives  91.8 us (20%)
  starting transfers between devices  42.1 us (9%)
  matrix products  25.5 us (6%)
  local copies, waits for them, and re-layouts  22.6 us (5%)
  other arithmetic  8.09 us (2%)
    all_to_all x1, waiting for transfers between devices, local(): lax.all_to_all(jnp.stack([packed[None]] * lax.axis_size(EP)), EP, 0, 0)  128 us
    all_to_all x1, blocking collectives, local(): lax.all_to_all(spread, ('rep',) + EP, 0, 0, tiled=True).reshape(-1, chunk)  37.8 us
    all_to_all x1, blocking collectives, local(): parts = lax.all_to_all(parts, 'rep', 0, 0, tiled=True)  31.3 us
    all_to_all x1, waiting for transfers between devices, local(): back = lax.all_to_all(out_cols, ('rep',) + EP, 0, 0, tiled=True)  27.8 us
    all_to_all x1, waiting for transfers between devices, local(): lax.all_to_all(w_gate[0].reshape(rep_count, chunk, hidden_width), 'rep',...  23.1 us
    all_to_all x1, waiting for transfers between devices, local(): down_cols = lax.all_to_all(down_cols, 'rep', 0, 0, tiled=True)  23.1 us
    all_to_all x1, waiting for transfers between devices, local(): lax.all_to_all(w_up[0].reshape(rep_count, chunk, hidden_width), 'rep', 0,...  22.8 us
    all_to_all x1, waiting for transfers between devices, local(): lax.all_to_all(partial, 'epo', 0, 0, tiled=True).astype(jnp.float32)  22.7 us
  transfers between devices with their start and end apart: 7, of which 7 were waited for; matrix products, arithmetic and copies ran while one was open for 3% of the time, Pallas kernels for 0%

profile of v1, /device:TPU:1, one launch (start us, length us, event | category | flops | bytes accessed | tf_op | source)
XLA Modules:
  0.0 449.4 jit_solution(15101662592000451585)
XLA Ops:
  4.5 7.5 %all-to-all-start = ((bf16[8,2,18432]{2,1,0:T(2,128)(2,1)}), bf16[8,2,18432]{2,1,0:T(2,128)(2,1)S(1)}, u32[]{:S(2)}, u32[]{:S(2)}) async-start(bf16[8,2,18432]{2,1,0:T(2,128)(2,1)} %reshape.266), calls=%async_computation | async-start | bytes 1179648 | tf_op jit(solution)/shard_map/all_to_all | solution.py:67
  12.3 1.5 copy.150
  13.9 10.5 %all-to-all-done = bf16[8,2,18432]{2,1,0:T(2,128)(2,1)S(1)} async-done(((bf16[8,2,18432]{2,1,0:T(2,128)(2,1)}), bf16[8,2,18432]{2,1,0:T(2,128)(2,1)S(1)}, u32[]{:S(2)}, u32[]{:S(2)}) %all-to-all-start) | async-done | bytes 589856 | tf_op jit(solution)/shard_map/all_to_all | solution.py:67
  24.4 4.3 all-to-all-start.2
  28.7 2.7 copy.115
  31.4 23.1 %all-to-all-done.2 = bf16[8,128,896]{2,1,0:T(8,128)(2,1)} async-done(((bf16[8,128,896]{2,1,0:T(8,128)(2,1)}), bf16[8,128,896]{2,1,0:T(8,128)(2,1)}, u32[]{:S(2)}, u32[]{:S(2)}) %all-to-all-start.2) | async-done | bytes 1835040 | tf_op jit(solution)/shard_map/all_to_all | solution.py:100
  54.5 4.3 all-to-all-start.3
  58.8 2.6 copy.116
  61.5 23.1 %all-to-all-done.3 = bf16[8,896,128]{1,2,0:T(8,128)(2,1)} async-done(((bf16[8,896,128]{1,2,0:T(8,128)(2,1)}), bf16[8,896,128]{1,2,0:T(8,128)(2,1)}, u32[]{:S(2)}, u32[]{:S(2)}) %all-to-all-start.3) | async-done | bytes 1835040 | tf_op jit(solution)/shard_map/all_to_all | solution.py:101
  84.6 4.3 all-to-all-start.4
  91.8 22.8 %all-to-all-done.4 = bf16[8,896,128]{1,2,0:T(8,128)(2,1)} async-done(((bf16[8,896,128]{1,2,0:T(8,128)(2,1)}), bf16[8,896,128]{1,2,0:T(8,128)(2,1)}, u32[]{:S(2)}, u32[]{:S(2)}) %all-to-all-start.4) | async-done | bytes 1835040 | tf_op jit(solution)/shard_map/all_to_all | solution.py:104
  114.7 3.0 stack.3
  117.7 9.7 %all-to-all-start.1 = ((bf16[32,1,144,576]{3,2,1,0:T(8,128)(2,1)}), bf16[32,1,144,576]{3,2,1,0:T(8,128)(2,1)}, u32[]{:S(2)}, u32[]{:S(2)}) async-start(bf16[32,1,144,576]{3,2,1,0:T(8,128)(2,1)} %stack.3), calls=%async_computation.1 | async-start | bytes 11796480 | tf_op jit(solution)/shard_map/all_to_all | solution.py:94
  128.7 3.9 fusion.11
  132.6 128.2 %all-to-all-done.1 = bf16[32,1,144,576]{3,2,1,0:T(8,128)(2,1)} async-done(((bf16[32,1,144,576]{3,2,1,0:T(8,128)(2,1)}), bf16[32,1,144,576]{3,2,1,0:T(8,128)(2,1)}, u32[]{:S(2)}, u32[]{:S(2)}) %all-to-all-start.1) | async-done | bytes 5308448 | tf_op jit(solution)/shard_map/all_to_all | solution.py:94
  260.7 4.7 %fusion.57 = (f32[2,128]{1,0:T(2,128)S(1)}, f32[2,128,4608]{1,2,0:T(8,128)S(1)}) fusion(bf16[4608,576,1]{1,0,2:T(8,128)(2,1)} %bitcast.13, bf16[128,2,576]{0,2,1:T(8,128)(2,1)S(1)} %bitcast.107, pred[128,4608]{0,1:T(8,128)(4,1)S(1)} %fusion.11), kind=kOutput, calls=%fused_computation.92 | convolution fusion | flops 1362493184 | bytes 10912768 | tf_op jit(solution)/shard_map/thc,kc->htk/dot_general | solution.py:120
  266.1 1.5 copy-done.2
  267.6 5.5 %fusion.17 = bf16[128,2,128]{2,0,1:T(8,128)(2,1)S(1)} fusion(bf16[2,512,128]{2,1,0:T(8,128)(2,1)S(1)} %copy-done.11, f32[2,128,4608]{1,2,0:T(8,128)} %copy-done.2, f32[2,128]{1,0:T(2,128)S(1)} %get-tuple-element.13, bf16[4608,576]{1,0:T(8,128)(2,1)} %bitcast.10, f32[128,2]{0,1:T(2,128)S(1)} %bitcast.111), kind=kOutput, calls=%fused_computation.31 | convolution fusion | flops 1244168192 | bytes 9766912 | tf_op jit(solution)/shard_map/thc,hcv->thv/dot_general | solution.py:131
  273.3 2.7 convolution_convert_fusion.2
  276.0 5.3 %all_to_all.55 = bf16[2,64,7168]{2,1,0:T(8,128)(2,1)S(1)} all-to-all(bf16[2,64,7168]{2,1,0:T(8,128)(2,1)S(1)} %convolution_convert_fusion.2), channel_id=1, replica_groups=mesh['rep'=8,'epo'=16,'core'=2] {'core'}, dimensions={0} | all-to-all | bytes 3670016 | tf_op jit(solution)/shard_map/all_to_all | solution.py:138
  282.2 1.5 convert_element_type.105
  283.8 3.6 all-to-all-start.6
  288.1 22.7 %all-to-all-done.6 = bf16[16,16,1792]{2,1,0:T(8,128)(2,1)S(1)} async-done(((bf16[16,16,1792]{2,1,0:T(8,128)(2,1)}), bf16[16,16,1792]{2,1,0:T(8,128)(2,1)S(1)}, u32[]{:S(2)}, u32[]{:S(2)}) %all-to-all-start.6) | async-done | bytes 917536 | tf_op jit(solution)/shard_map/all_to_all | solution.py:142
  313.2 37.8 %all_to_all.56 = bf16[256,2,896]{2,1,0:T(2,128)(2,1)S(1)} all-to-all(bf16[256,2,896]{2,1,0:T(2,128)(2,1)S(1)} %copy.126), channel_id=1, replica_groups=mesh['rep'=8,'epo'=16,'core'=2] {'rep','epo','core'}, dimensions={0} | all-to-all | bytes 1835008 | tf_op jit(solution)/shard_map/all_to_all | solution.py:176
  351.3 2.8 fusion.12
  354.1 2.8 fusion.13
  357.1 31.3 %all_to_all.57 = bf16[8,512,256]{1,2,0:T(8,128)(2,1)S(1)} all-to-all(bf16[8,512,256]{1,2,0:T(8,128)(2,1)S(1)} %pad_maximum_fusion), channel_id=1, replica_groups=mesh['rep'=8,'epo'=16,'core'=2] {'rep'}, dimensions={0} | all-to-all | bytes 4194304 | tf_op jit(solution)/shard_map/all_to_all | solution.py:180
  389.0 17.4 %all_to_all.58 = bf16[8,512,128]{2,1,0:T(8,128)(2,1)S(1)} all-to-all(bf16[8,512,128]{2,1,0:T(8,128)(2,1)S(1)} %broadcast_in_dim.17), channel_id=1, replica_groups=mesh['rep'=8,'epo'=16,'core'=2] {'rep'}, dimensions={0} | all-to-all | bytes 2097152 | tf_op jit(solution)/shard_map/all_to_all | solution.py:186
  406.3 3.6 convert_reduce_fusion
  410.0 1.3 reshape.251
  411.2 8.3 %all-to-all-start.10 = ((bf16[256,2,896]{2,1,0:T(2,128)(2,1)}), bf16[256,2,896]{2,1,0:T(2,128)(2,1)S(1)}, u32[]{:S(2)}, u32[]{:S(2)}) async-start(bf16[256,2,896]{2,1,0:T(2,128)(2,1)} %reshape.251), calls=%async_computation.10 | async-start | bytes 1835008 | tf_op jit(solution)/shard_map/all_to_all | solution.py:191
  419.9 27.8 %all-to-all-done.10 = bf16[256,2,896]{2,1,0:T(2,128)(2,1)S(1)} async-done(((bf16[256,2,896]{2,1,0:T(2,128)(2,1)}), bf16[256,2,896]{2,1,0:T(2,128)(2,1)S(1)}, u32[]{:S(2)}, u32[]{:S(2)}) %all-to-all-start.10) | async-done | bytes 917536 | tf_op jit(solution)/shard_map/all_to_all | solution.py:191
  (90 shorter events, 16.0 us)
Async XLA Ops:
  0.0 1.3 copy-start
  1.4 10.6 %copy-start.3 = (bf16[1,128,7168]{2,1,0:T(8,128)(2,1)S(1)}, bf16[1,128,7168]{2,1,0:T(8,128)(2,1)}, u32[]{:S(2)}) copy-start(bf16[1,128,7168]{2,1,0:T(8,128)(2,1)} %param.29) | copy-start | bytes 5505028
  4.5 19.9 %all-to-all-start = ((bf16[8,2,18432]{2,1,0:T(2,128)(2,1)}), bf16[8,2,18432]{2,1,0:T(2,128)(2,1)S(1)}, u32[]{:S(2)}, u32[]{:S(2)}) async-start(bf16[8,2,18432]{2,1,0:T(2,128)(2,1)} %reshape.266), calls=%async_computation | async-start | bytes 1179648 | tf_op jit(solution)/shard_map/all_to_all | solution.py:67
  13.8 14.9 %copy-start.4 = (bf16[1,7168,128]{2,1,0:T(8,128)(2,1)S(1)}, bf16[1,7168,128]{2,1,0:T(8,128)(2,1)}, u32[]{:S(2)}) copy-start(bf16[1,7168,128]{2,1,0:T(8,128)(2,1)} %param.27) | copy-start | bytes 5505028
  24.4 30.1 %all-to-all-start.2 = ((bf16[8,128,896]{2,1,0:T(8,128)(2,1)}), bf16[8,128,896]{2,1,0:T(8,128)(2,1)}, u32[]{:S(2)}, u32[]{:S(2)}) async-start(bf16[8,128,896]{2,1,0:T(8,128)(2,1)} %bitcast.95), calls=%async_computation.2 | async-start | bytes 3670016 | tf_op jit(solution)/shard_map/all_to_all | solution.py:100
  31.4 27.4 %copy-start.5 = (bf16[1,7168,128]{2,1,0:T(8,128)(2,1)S(1)}, bf16[1,7168,128]{2,1,0:T(8,128)(2,1)}, u32[]{:S(2)}) copy-start(bf16[1,7168,128]{2,1,0:T(8,128)(2,1)} %param.28) | copy-start | bytes 5505028
  54.5 30.1 %all-to-all-start.3 = ((bf16[8,896,128]{1,2,0:T(8,128)(2,1)}), bf16[8,896,128]{1,2,0:T(8,128)(2,1)}, u32[]{:S(2)}, u32[]{:S(2)}) async-start(bf16[8,896,128]{1,2,0:T(8,128)(2,1)} %copy.115), calls=%async_computation.3 | async-start | bytes 3670016 | tf_op jit(solution)/shard_map/all_to_all | solution.py:101
  61.5 28.3 %copy-start.9 = (bf16[1,2304]{1,0:T(2,128)(2,1)S(1)}, bf16[1,2304]{1,0:T(2,128)(2,1)}, u32[]{:S(2)}) copy-start(bf16[1,2304]{1,0:T(2,128)(2,1)} %param.16) | copy-start | bytes 13828
  84.6 30.1 %all-to-all-start.4 = ((bf16[8,896,128]{1,2,0:T(8,128)(2,1)}), bf16[8,896,128]{1,2,0:T(8,128)(2,1)}, u32[]{:S(2)}, u32[]{:S(2)}) async-start(bf16[8,896,128]{1,2,0:T(8,128)(2,1)} %copy.116), calls=%async_computation.4 | async-start | bytes 3670016 | tf_op jit(solution)/shard_map/all_to_all | solution.py:104
  117.7 10.7 %copy-start.7 = (bf16[1,128,1152]{2,1,0:T(8,128)(2,1)S(1)}, bf16[1,128,1152]{2,1,0:T(8,128)(2,1)}, u32[]{:S(2)}) copy-start(bf16[1,128,1152]{2,1,0:T(8,128)(2,1)} %param.15) | copy-start | bytes 884740
  117.7 143.0 %all-to-all-start.1 = ((bf16[32,1,144,576]{3,2,1,0:T(8,128)(2,1)}), bf16[32,1,144,576]{3,2,1,0:T(8,128)(2,1)}, u32[]{:S(2)}, u32[]{:S(2)}) async-start(bf16[32,1,144,576]{3,2,1,0:T(8,128)(2,1)} %stack.3), calls=%async_computation.1 | async-start | bytes 11796480 | tf_op jit(solution)/shard_map/all_to_all | solution.py:94
  265.4 2.2 copy-start.2
  265.5 2.2 copy-start.11
  282.2 5.2 %copy-start.6 = (bf16[1,4,7168]{2,1,0:T(4,128)(2,1)S(1)}, bf16[1,4,7168]{2,1,0:T(4,128)(2,1)}, u32[]{:S(2)}) copy-start(bf16[1,4,7168]{2,1,0:T(4,128)(2,1)} %param.21) | copy-start | bytes 172036
  282.2 5.3 %copy-start.10 = (s32[1,4,8]{2,1,0:T(4,128)S(1)}, s32[1,4,8]{2,1,0:T(4,128)}, u32[]{:S(2)}) copy-start(s32[1,4,8]{2,1,0:T(4,128)} %param.25) | copy-start | bytes 388
  282.2 5.5 %copy-start.8 = (bf16[7168]{0:T(1024)(128)(2,1)S(1)}, bf16[7168]{0:T(1024)(128)(2,1)}, u32[]{:S(2)}) copy-start(bf16[7168]{0:T(1024)(128)(2,1)} %param.24) | copy-start | bytes 43012
  283.8 27.1 %all-to-all-start.6 = ((bf16[16,16,1792]{2,1,0:T(8,128)(2,1)}), bf16[16,16,1792]{2,1,0:T(8,128)(2,1)S(1)}, u32[]{:S(2)}, u32[]{:S(2)}) async-start(bf16[16,16,1792]{2,1,0:T(8,128)(2,1)} %convert_element_type.105), calls=%async_computation.6 | async-start | bytes 1835008 | tf_op jit(solution)/shard_map/all_to_all | solution.py:142
  410.0 9.6 %copy-start.12 = (bf16[1,4,8]{2,1,0:T(4,128)(2,1)S(1)}, bf16[1,4,8]{2,1,0:T(4,128)(2,1)}, u32[]{:S(2)}) copy-start(bf16[1,4,8]{2,1,0:T(4,128)(2,1)} %param.26) | copy-start | bytes 196
  411.2 36.5 %all-to-all-start.10 = ((bf16[256,2,896]{2,1,0:T(2,128)(2,1)}), bf16[256,2,896]{2,1,0:T(2,128)(2,1)S(1)}, u32[]{:S(2)}, u32[]{:S(2)}) async-start(bf16[256,2,896]{2,1,0:T(2,128)(2,1)} %reshape.251), calls=%async_computation.10 | async-start | bytes 1835008 | tf_op jit(solution)/shard_map/all_to_all | solution.py:191
  447.8 1.6 copy-start.1
